TPU v7x, 128 devices: a whole 4x4x4 slice. The times are simulated.
128 devices in a mesh: seq: 16 (over z, x), head: 8 (over y, core).
Axes of the slice: x: 4, y: 4, z: 4, core: 2. Of those that a mesh axis runs over, the one named last changes fastest.
Arguments:
- inputs: bfloat16 [16384, 8192], P('seq', 'head'), as said below
- gate_input: bfloat16 [16384, 8192], P('seq', 'head'), may hold values from -6 to 6
- log_decay: float32 [16384, 128], P('seq', 'head'), as said below
- b_matrix: bfloat16 [16384, 8, 128], P('seq', 'head'), may hold values from -6 to 6
- c_matrix: bfloat16 [16384, 8, 128], P('seq', 'head'), may hold values from -1.25 to 1.25
- norm_gain: float32 [8192], P('head'), may hold values from 0.1 to 1.9
- cotangent: bfloat16 [16384, 8192], P('seq', 'head'), may hold values from -6 to 6
Outputs:
- normed: bfloat16 [16384, 8192], P('seq', 'head')
- grad_inputs: bfloat16 [16384, 8192], P('seq', 'head')
- grad_gate: bfloat16 [16384, 8192], P('seq', 'head')
- grad_decay: float32 [16384, 128], P('seq', 'head')
- grad_b_matrix: float32 [16384, 8, 128], P('seq', 'head')
- grad_c_matrix: float32 [16384, 8, 128], P('seq', 'head')
Inputs may be any that keep to these rules, and one draw needn't show every extreme that they name: `log_decay`: every entry is strictly negative. `inputs`: real-valued and finite.
All inputs are finite; a program needn't handle non-finite values.
Results may differ from a plain program's by a relative error of at most 0.003.
Values sent between devices are 32-bit elements; how exact they have to be, the bound alone decides.
No kernel may reach another device: no remote copies, remote signals or barrier semaphores. Data moves between devices by JAX's collectives and lax.ppermute only.
A program may use at most 192 MiB of HBM per device.

v0:
```python
import jax
import jax.numpy as jnp
from jax import lax
from jax.sharding import PartitionSpec as P


SPAN = 128


PRECISION = lax.Precision.HIGH
EPSILON = 1e-05


def shard_weights(log_carry, reverse):
    count = lax.axis_size("seq")
    place = lax.axis_index("seq")
    ids = jnp.arange(count)
    if reverse:
        source_ok = ids > place
        between = (ids[None, :] > place) & (ids[None, :] < ids[:, None])
    else:
        source_ok = ids < place
        between = (ids[None, :] > ids[:, None]) & (ids[None, :] < place)
    log_gap = jnp.sum(jnp.where(between[:, :, None, None], log_carry[None], 0.0), axis=1)
    return jnp.where(source_ok[:, None, None], jnp.exp(log_gap), 0.0)


def weighted_sum(weights, states):
    total = weights[0][..., None, None] * states[0]
    for source in range(1, states.shape[0]):
        total = total + weights[source][..., None, None] * states[source]
    return total


def pair_scores(c_half, b_half):
    return jnp.einsum("kign,kjgn->kgij", c_half, b_half, preferred_element_type=jnp.float32)


def score_grads(grad_scores, b_blocks, c_blocks):
    grad_c = jnp.einsum("kgij,kjgn->kign", grad_scores, b_blocks, precision=PRECISION)
    grad_b = jnp.einsum("kgij,kign->kjgn", grad_scores, c_blocks, precision=PRECISION)
    return (grad_b, grad_c)


def span_core(x_blocks, a_blocks, b_blocks, c_blocks, scores):
    running = jnp.cumsum(jnp.moveaxis(a_blocks, 1, 3), axis=3)
    length = running.shape[3]
    row_numbers = lax.broadcasted_iota(jnp.int32, (length, length), 0)
    col_ids = lax.broadcasted_iota(jnp.int32, (length, length), 1)
    causal = row_numbers >= col_ids
    log_gaps = running[..., :, None] - running[..., None, :]
    decays = jnp.exp(jnp.where(causal, log_gaps, -1e30))
    weighted = decays * scores[:, :, None]
    diagonal = jnp.einsum("kgrij,kjgrp->kigrp", weighted, x_blocks, precision=PRECISION)
    span_end = running[..., -1]
    to_end = jnp.exp(span_end[..., None] - running)
    scaled = x_blocks * jnp.moveaxis(to_end, 3, 1)[..., None]
    block_states = jnp.einsum("kjgrp,kjgn->kgrpn", scaled, b_blocks, precision=PRECISION)

    factors = jnp.exp(span_end)
    carried = jnp.zeros(block_states.shape[1:], jnp.float32)
    start_list = []
    for block in range(block_states.shape[0]):
        start_list.append(carried)
        carried = factors[block][..., None, None] * carried + block_states[block]
    final = carried
    starts = jnp.stack(start_list)
    from_state = jnp.einsum("kign,kgrpn->kigrp", c_blocks, starts, precision=PRECISION)
    ssd_out = diagonal + from_state * jnp.moveaxis(jnp.exp(running), 3, 1)[..., None]
    return (ssd_out, final, running, span_end)


def local_core(x_blocks, a_blocks, b_blocks, c_blocks, scores):
    ssd_part, final, running, span_end = span_core(x_blocks, a_blocks, b_blocks, c_blocks, scores)
    earlier = jnp.cumsum(span_end, axis=0) - span_end
    reach = jnp.exp(running + earlier[..., None])
    log_carry = jnp.sum(span_end, axis=0)
    return (ssd_part, final, reach, jnp.exp(log_carry), log_carry)


def add_incoming(ssd_part, final, reach, carry_all, c_blocks, incoming):
    projected = jnp.einsum("kign,grpn->kigrp", c_blocks, incoming, precision=PRECISION)
    from_left = projected * jnp.moveaxis(reach, 3, 1)[..., None]
    return (ssd_part + from_left, carry_all[..., None, None] * incoming + final)


def device_body(inputs, gate_input, log_decay, b_matrix, c_matrix, norm_gain, cotangent):
    tok_rows, width = inputs.shape
    head_count = log_decay.shape[1]
    groups = b_matrix.shape[1]
    state_size = b_matrix.shape[2]
    head_size = width // head_count
    per_group = head_count // groups
    blocks = tok_rows // SPAN
    full_width = width * lax.axis_size("head")
    x_blocks = inputs.astype(jnp.float32).reshape(blocks, SPAN, groups, per_group, head_size)
    a_blocks = log_decay.reshape(blocks, SPAN, groups, per_group)
    b_half = b_matrix.reshape(blocks, SPAN, groups, state_size)
    c_half = c_matrix.reshape(blocks, SPAN, groups, state_size)
    b_blocks = b_half.astype(jnp.float32)
    c_blocks = c_half.astype(jnp.float32)
    scores = pair_scores(c_half, b_half)
    core_out, core_pull = jax.vjp(local_core, x_blocks, a_blocks, b_blocks, c_blocks, scores)
    ssd_part, final, reach, carry_all, log_carry = core_out
    ssd_part = lax.optimization_barrier(ssd_part)
    log_rows = jnp.broadcast_to(log_carry[..., None, None], final.shape[:2] + (8, final.shape[3]))
    packed = lax.all_gather(jnp.concatenate([final, log_rows], axis=2), "seq")
    head_size_p = final.shape[2]
    gathered_log = jnp.max(packed[:, :, :, head_size_p:], axis=(3, 4))
    incoming = weighted_sum(shard_weights(gathered_log, False), packed)[:, :, :head_size_p]

    def light_step(part_a, part_b, part_c, part_d, part_e):
        return add_incoming(part_a, part_b, part_c, part_d, part_e, incoming)

    light_out, light_pull = jax.vjp(light_step, ssd_part, final, reach, carry_all, c_blocks)
    ssd_out = light_out[0].reshape(tok_rows, width)
    gate_value = gate_input.astype(jnp.float32)
    sigmoid_gate = jax.nn.sigmoid(gate_value)
    gate_silu = gate_value * sigmoid_gate
    gated = ssd_out * gate_silu
    scaled_cot = norm_gain[None, :] * cotangent.astype(jnp.float32)
    squares, products = lax.psum(
        (jnp.sum(gated * gated, axis=1), jnp.sum(gated * scaled_cot, axis=1)), "head"
    )
    inverse_rms = lax.rsqrt(squares / full_width + EPSILON)
    normed = (gated * inverse_rms[:, None] * norm_gain[None, :]).astype(jnp.bfloat16)
    grad_gated = (
        inverse_rms[:, None] * scaled_cot
        - gated * (inverse_rms**3 * products / full_width)[:, None]
    )
    grad_gate = (
        grad_gated * ssd_out * sigmoid_gate * (1.0 + gate_value * (1.0 - sigmoid_gate))
    ).astype(jnp.bfloat16)
    grad_ssd = grad_gated * gate_silu
    upstream = grad_ssd.reshape(blocks, SPAN, groups, per_group, head_size)
    reached = upstream * jnp.moveaxis(reach, 3, 1)[..., None]
    leaving = jnp.einsum("kign,kigrp->grpn", c_blocks, reached, precision=PRECISION)
    gathered_leaving = lax.all_gather(leaving, "seq")
    adjoint = weighted_sum(shard_weights(gathered_log, True), gathered_leaving)
    light_grads = light_pull((upstream, adjoint))
    grad_x, grad_a, grad_b_core, grad_c_core, grad_scores = core_pull(
        tuple(light_grads[:4]) + (jnp.zeros_like(log_carry),)
    )
    extra_b, extra_c = score_grads(grad_scores, b_blocks, c_blocks)
    grad_b = grad_b_core + extra_b
    grad_c = grad_c_core + extra_c + light_grads[4]
    grad_inputs = grad_x.reshape(tok_rows, width).astype(jnp.bfloat16)
    grad_decay = grad_a.reshape(tok_rows, head_count)
    grad_b_matrix = grad_b.reshape(tok_rows, groups, state_size)
    grad_c_matrix = grad_c.reshape(tok_rows, groups, state_size)
    return (normed, grad_inputs, grad_gate, grad_decay, grad_b_matrix, grad_c_matrix)


def solution(mesh):
    placed = (
        P("seq", "head"),
        P("seq", "head"),
        P("seq", "head"),
        P("seq", "head", None),
        P("seq", "head", None),
        P("head"),
        P("seq", "head"),
    )
    return jax.shard_map(
        device_body,
        mesh=mesh,
        in_specs=placed,
        out_specs=(
            P("seq", "head"),
            P("seq", "head"),
            P("seq", "head"),
            P("seq", "head"),
            P("seq", "head", None),
            P("seq", "head", None),
        ),
        check_vma=False,
    )
```

profile of v0, /device:TPU:1, one launch (start us, length us, event | category | flops | bytes accessed | tf_op | source)
XLA Modules:
  0.0 277.5 jit_solution(11819874450475328405)
XLA Ops:
  7.2 0.9 copy.163
  8.1 2.3 reduce_window_sum.44
  10.4 0.8 fusion.160
  11.4 0.7 fusion.143
  12.1 4.2 %copy.113 = f32[1024,1024]{0,1:T(8,128)} copy(bf16[1024,1024]{1,0:T(8,128)(2,1)} %param.7) | data formatting | bytes 6291456 | tf_op jit(solution)/shard_map/convert_element_type | solution.py:96
  16.3 3.2 %copy.164 = f32[128,8,8,128]{3,2,1,0:T(8,128)S(1)} copy(f32[128,8,8,128]{3,1,2,0:T(8,128)} %bitcast.602) | data formatting | bytes 8388608
  19.8 0.4 broadcast_multiply_fusion.1
  20.2 0.5 copy-done.27
  20.7 1.6 fusion.49
  22.4 1.9 copy-done.6
  24.3 1.6 slice_add_fusion.8
  26.0 0.9 pad_maximum_fusion
  27.2 4.0 %reshape.1666 = bf16[8,128,16,64]{3,2,1,0:T(8,128)(2,1)} reshape(bf16[1024,1024]{1,0:T(8,128)(2,1)S(1)} %copy-done.7) | data formatting | bytes 4194304 | tf_op jit(solution)/shard_map/reshape.7
  31.2 5.8 %copy.112 = bf16[8,128,16,64]{1,3,2,0:T(8,128)(2,1)} copy(bf16[8,128,16,64]{3,2,1,0:T(8,128)(2,1)} %reshape.1666) | data formatting | bytes 4194304 | tf_op jit(solution)/shard_map/reshape.7
  37.1 1.2 bitcast_dynamic-update-slice_fusion.6
  38.4 1.1 bitcast_dynamic-update-slice_fusion.4
  39.5 1.1 bitcast_dynamic-update-slice_fusion.3
  41.1 1.3 fusion.30
  42.4 0.4 copy-done.4
  43.1 1.8 copy-done.11
  44.9 8.1 %bitcast_add_fusion.1 = f32[8,128,1,16,64]{1,4,3,0,2:T(8,128)} fusion(f32[8,16,64,128]{3,2,1,0:T(8,128)S(1)} %fusion.30, f32[8,128,16]{1,2,0:T(8,128)S(1)} %copy-done.31, bf16[8,128,16,64]{1,3,2,0:T(8,128)(2,1)S(1)} %copy-done.30, f32[8,128,128]{2,1,0:T(8,128)S(1)} %fusion.163, f32[8,16,128]{2,1,0:T(8,128)S(1)} %bitcast.608, ...), kind=kOutput, calls=%fused_computation.24 | convolution fusion | flops 813694976 | bytes 11157504 | tf_op jit(solution)/shard_map/jvp(kgrij,kjgrp->kigrp)/dot_general | solution.py:54
  53.0 3.9 %copy.118 = bf16[1024,1024]{0,1:T(8,128)(2,1)} copy(bf16[1024,1024]{1,0:T(8,128)(2,1)} %param.8) | data formatting | bytes 4194304 | tf_op args[1]
  56.9 3.9 %copy.119 = bf16[1024,1024]{0,1:T(8,128)(2,1)} copy(bf16[1024,1024]{1,0:T(8,128)(2,1)} %param.13) | data formatting | bytes 4194304 | tf_op args[6]
  60.9 0.7 copy.120
  61.6 44.3 %all-gather.5.cloned.1.call-done = f32[16,16,72,128]{3,2,1,0:T(8,128)} async-done(((f32[1,16,72,128]{3,2,1,0:T(8,128)}), f32[16,16,72,128]{3,2,1,0:T(8,128)}) %all-gather.5.cloned.1.call-update) | async-done | bytes 9437200 | tf_op jit(solution)/shard_map/all_gather | solution.py:107
  105.9 1.7 slice_reduce_fusion
  107.8 2.2 slice_multiply_fusion
  110.0 3.3 %fusion.90 = f32[1,16,72,128]{3,2,1,0:T(8,128)S(1)} fusion(f32[16,16,72,128]{3,2,1,0:T(8,128)} %all-gather.5.cloned.1.call-done, f32[16]{0:T(128)S(1)} %get-tuple-element.112, f32[16]{0:T(128)S(1)} %get-tuple-element.113, f32[16]{0:T(128)S(1)} %get-tuple-element.114, f32[16]{0:T(128)S(1)} %get-tuple-element.115, f32[16]{0:T(128)S(1)} %get-tuple-element.116, ...), kind=kLoop, calls=%fused_computation.95 | loop fusion | flops 2801664 | bytes 6488704 | tf_op jit(solution)/shard_map/add | solution.py:31
  113.5 0.4 copy-done.26
  113.9 3.6 %fusion.23 = (f32[8,128,1,16,64]{1,4,3,0,2:T(8,128)S(1)}, f32[16,64,8,128]{3,1,0,2:T(8,128)}) fusion(f32[8,128,1,16,64]{1,4,3,0,2:T(8,128)S(1)} %copy-done.26, f32[8,128,16]{1,2,0:T(8,128)S(1)} %get-tuple-element.86, bf16[8,128,128,1]{2,1,3,0:T(8,128)(2,1)S(1)} %bitcast.585, f32[1,16,64,128]{3,2,1,0:T(8,128)S(1)} %fusion.99), kind=kOutput, calls=%fused_computation.37 | convolution fusion | flops 807403520 | bytes 13434880 | tf_op jit(solution)/shard_map/jvp(kign,grpn->kigrp)/dot_general | solution.py:82
  117.5 3.3 %copy.117 = f32[8,128,1,16,64]{1,0,4,3,2:T(8,128)S(1)} copy(f32[8,128,1,16,64]{1,4,3,0,2:T(8,128)S(1)} %get-tuple-element.124) | data formatting | bytes 8388608 | tf_op jit(solution)/shard_map/jvp()/add | solution.py:84
  120.9 3.4 %multiply_reduce_fusion.1 = (f32[1024]{0:T(1024)}, f32[1024]{0:T(1024)}) fusion(bf16[1024,1024]{0,1:T(8,128)(2,1)S(1)} %copy-done.9, f32[1024]{0:T(1024)S(1)} %copy-done.40, bf16[1024,1024]{0,1:T(8,128)(2,1)S(1)} %copy-done.8, f32[128,8,8,128]{3,2,1,0:T(8,128)S(1)} %bitcast.597), kind=kLoop, calls=%fused_computation.52 | loop fusion | flops 12580864 | bytes 8400896 | tf_op jit(solution)/shard_map/reduce_sum | solution.py:123
  124.3 13.9 %all-reduce.17 = (f32[1024]{0:T(1024)}, f32[1024]{0:T(1024)}) all-reduce(f32[1024]{0:T(1024)} %get-tuple-element.34, f32[1024]{0:T(1024)} %get-tuple-element.33), channel_id=1, replica_groups=mesh['seq'=16,'head'=8] {'head'}, use_global_device_ids=true, to_apply=%region_6.7 | all-reduce | flops 2048 | bytes 16384 | tf_op jit(solution)/shard_map/psum | solution.py:122
  138.1 0.7 fusion.152
  138.8 7.2 %fusion.12 = (bf16[1024,1024]{0,1:T(8,128)(2,1)}, f32[128,8,8,128]{3,1,2,0:T(8,128)S(1)}, bf16[1024,1024]{0,1:T(8,128)(2,1)}) fusion(bf16[1024,1024]{0,1:T(8,128)(2,1)} %copy.118, f32[128,8,8,128]{3,2,1,0:T(8,128)} %bitcast.598, bf16[1024,1024]{0,1:T(8,128)(2,1)} %copy.119, f32[1024]{0:T(1024)S(1)} %get-tuple-element.122, f32[1024]{0:T(1024)} %param.12, ...), kind=kLoop, calls=%fused_computation.16 | loop fusion | flops 23068672 | bytes 16789504 | tf_op jit(solution)/shard_map/convert_element_type | solution.py:133
  146.0 1.0 copy.166
  147.1 0.4 broadcast_multiply_fusion
  147.4 1.6 copy-done.1
  149.0 2.1 fusion.65
  151.1 4.4 %reshape.1665 = f32[8,128,1,16,64]{4,3,1,0,2:T(8,128)} reshape(bf16[1024,1024]{1,0:T(8,128)(2,1)S(1)} %copy-done.7) | data formatting | bytes 6291456 | tf_op jit(solution)/shard_map/reshape | solution.py:96
  155.5 7.2 %copy.128 = f32[8,128,1,16,64]{1,4,3,0,2:T(8,128)} copy(f32[8,128,1,16,64]{4,3,1,0,2:T(8,128)} %reshape.1665) | data formatting | bytes 8388608 | tf_op jit(solution)/shard_map/reshape | solution.py:96
  162.8 4.1 %copy.144 = bf16[1024,1024]{1,0:T(8,128)(2,1)} copy(bf16[1024,1024]{0,1:T(8,128)(2,1)} %get-tuple-element.85) | data formatting | bytes 4194304
  166.9 2.5 copy.146
  169.4 13.2 %fusion.6 = (f32[8,16,128]{2,1,0:T(8,128)}, f32[8,16,128]{2,1,0:T(8,128)}, f32[8,128,128]{2,1,0:T(8,128)S(1)}) fusion(f32[8,128,128]{2,1,0:T(8,128)} %copy-done.33, f32[8,16,128]{2,1,0:T(8,128)S(1)} %bitcast.609, pred[128,128]{1,0:T(8,128)(4,1)} %copy-done.42, bf16[8,128,16,64]{1,3,2,0:T(8,128)(2,1)} %copy.112, f32[8,16,64,128]{3,0,2,1:T(8,128)} %bitcast.591), kind=kOutput, calls=%fused_computation.10 | convolution fusion | flops 824016896 | bytes 7553024 | tf_op jit(solution)/shard_map/transpose(jvp(kgrij,kjgrp->kigrp))/dot_general | solution.py:54
  183.2 3.9 %fusion.85 = f32[8,128,1,128]{3,1,0,2:T(8,128)S(1)} fusion(f32[8,128,1,128]{3,1,0,2:T(8,128)S(1)} %convolution_bitcast_fusion, f32[8,1,16,64,128]{4,3,2,1,0:T(8,128)S(1)} %copy-done.5, f32[8,128,1,16,64]{1,0,4,3,2:T(8,128)S(1)} %bitcast.593, f32[8,128,16]{1,2,0:T(8,128)S(1)} %copy-done.32), kind=kOutput, calls=%fused_computation.90 | convolution fusion | flops 806486016 | bytes 9502720 | tf_op jit(solution)/shard_map/transpose(jvp(kign,kgrpn->kigrp))/dot_general | solution.py:68
  187.0 4.3 %fusion.81 = f32[8,128,1,128]{3,1,0,2:T(8,128)} fusion(f32[8,128,1,128]{3,1,0,2:T(8,128)S(1)} %fusion.85, f32[8,128,1,16,64]{1,0,4,3,2:T(8,128)S(1)} %bitcast.594, f32[8,128,16]{1,2,0:T(8,128)S(1)} %get-tuple-element.86, f32[1,16,64,128]{3,2,1,0:T(8,128)S(1)} %fusion.99), kind=kOutput, calls=%fused_computation.88 | convolution fusion | flops 806486016 | bytes 5832704 | tf_op jit(solution)/shard_map/transpose(jvp(kign,grpn->kigrp))/dot_general | solution.py:82
  191.3 3.8 %fusion.19 = f32[8,16,64,128]{3,2,1,0:T(8,128)} fusion(bf16[8,128,128,1]{2,1,3,0:T(8,128)(2,1)S(1)} %bitcast.586, f32[8,128,1,16,64]{1,0,4,3,2:T(8,128)S(1)} %bitcast.595, f32[8,128,16]{1,2,0:T(8,128)S(1)} %copy-done.32), kind=kOutput, calls=%fused_computation.27 | convolution fusion | flops 806354944 | bytes 8716288 | tf_op jit(solution)/shard_map/transpose(jvp(kign,kgrpn->kigrp))/dot_general | solution.py:68
  195.1 1.3 copy-done.12
  196.3 3.2 %fusion.24 = (f32[8,128,16]{1,2,0:T(8,128)S(1)}, f32[8,128,16]{1,2,0:T(8,128)}) fusion(f32[16,64,8,128]{3,1,0,2:T(8,128)S(1)} %copy-done.10, f32[8,128,1,16,64]{1,0,4,3,2:T(8,128)S(1)} %bitcast.596, f32[8,16,64,128]{3,2,1,0:T(8,128)S(1)} %copy-done.12), kind=kLoop, calls=%fused_computation.38 | loop fusion | flops 4161536 | bytes 12713984 | tf_op jit(solution)/shard_map/transpose(jvp())/reduce_sum | solution.py:83
  199.5 21.7 %all-gather.7.cloned.1.call-done = f32[256,64,128]{2,1,0:T(8,128)} async-done(((f32[16,64,128]{2,1,0:T(8,128)}), f32[256,64,128]{2,1,0:T(8,128)}) %all-gather.7.cloned.1.call-update) | async-done | bytes 8388624 | tf_op jit(solution)/shard_map/all_gather | solution.py:138
  221.4 4.6 %multiply_reduce_fusion.11 = (f32[16]{0:T(128)}, f32[16]{0:T(128)}, f32[1,16,64,128]{3,2,1,0:T(8,128)S(1)}) fusion(f32[1,16,64,128]{3,2,1,0:T(8,128)S(1)} %fusion.99, f32[1,16,64,128]{3,2,1,0:T(8,128)S(1)} %get-tuple-element.71, f32[256,64,128]{2,1,0:T(8,128)} %all-gather.7.cloned.1.call-done, f32[16]{0:T(128)S(1)} %get-tuple-element.91, ...), kind=kLoop, calls=%fused_computation.220 | loop fusion | flops 4587488 | bytes 9962624 | tf_op jit(solution)/shard_map/transpose(jvp())/reduce_sum | solution.py:84
  226.1 0.3 multiply_reduce_fusion.9
  226.8 0.8 copy-done.20
  228.7 1.5 multiply_reduce_fusion.4
  230.5 0.8 fusion.119
  231.3 1.4 copy-done.14
  232.7 3.6 %fusion.68 = f32[8,128,128]{1,2,0:T(8,128)S(1)} fusion(f32[8,128,16,64]{1,0,3,2:T(8,128)S(1)} %copy-done.14, f32[1,1,16,64,128]{4,3,2,1,0:T(8,128)S(1)} %fusion.147, f32[1,1,16,64,128]{4,3,2,1,0:T(8,128)S(1)} %bitcast.611, f32[1,1,16,64,128]{4,3,2,1,0:T(8,128)S(1)} %bitcast.613, f32[1,1,16,64,128]{4,3,2,1,0:T(8,128)S(1)} %bitcast.621, ...), kind=kOutput, calls=%fused_computation.83 | convolution fusion | flops 812646400 | bytes 8912896 | tf_op jit(solution)/shard_map/transpose(jvp(kjgrp,kjgn->kgrpn))/dot_general | solution.py:58
  236.3 1.3 fusion.84
  237.6 3.4 %fusion.21 = (f32[8,128,16]{1,2,0:T(8,128)S(1)}, f32[8,16,64,128]{3,2,1,0:T(8,128)}) fusion(f32[8,128,1,16,64]{1,4,3,0,2:T(8,128)S(1)} %copy-done.25, bf16[8,128,128,1]{2,1,3,0:T(8,128)(2,1)S(1)} %bitcast.607, f32[1,1,16,64,128]{4,3,2,1,0:T(8,128)S(1)} %fusion.147, f32[1,1,16,64,128]{4,3,2,1,0:T(8,128)S(1)} %bitcast.612, ...), kind=kOutput, calls=%fused_computation.31 | convolution fusion | flops 814727168 | bytes 12910592 | tf_op jit(solution)/shard_map/transpose(jvp(kjgrp,kjgn->kgrpn))/dot_general | solution.py:58
  241.6 9.9 %reduce_window_sum.47 = f32[8,1,16,128]{3,2,1,0:T(8,128)S(1)} reduce-window(f32[8,1,16,128]{3,2,1,0:T(8,128)S(1)} %fusion.141, f32[]{:T(128)} %constant.16.clone.1), window={size=1x1x1x128 pad=0_0x0_0x0_0x0_127}, to_apply=%region_27.28 | reduce-window | flops 2080768 | bytes 131076 | tf_op jit(solution)/shard_map/transpose(jvp(jit(cumsum)))/reduce_window_sum | solution.py:46
  251.6 0.6 copy.223
  252.2 7.5 %fusion.16 = bf16[8,128,1,16,64]{1,4,3,0,2:T(8,128)(2,1)S(1)} fusion(f32[8,16,64,128]{3,2,1,0:T(8,128)} %get-tuple-element.127, f32[8,128,16]{1,2,0:T(8,128)S(1)} %copy-done.37, f32[8,128,128]{2,1,0:T(8,128)} %copy-done.33, f32[8,16,128]{2,1,0:T(8,128)S(1)} %bitcast.610, pred[128,128]{1,0:T(8,128)(4,1)} %copy-done.42, f32[8,16,64,128]{3,0,2,1:T(8,128)} %bitcast.592), kind=kOutput, calls=%fused_computation.23 | convolution fusion | flops 814743552 | bytes 11157504 | tf_op jit(solution)/shard_map/transpose(jvp(kgrij,kjgrp->kigrp))/dot_general | solution.py:54
  259.7 4.3 %copy.157 = bf16[8,128,1,16,64]{4,3,1,0,2:T(8,128)(2,1)} copy(bf16[8,128,1,16,64]{1,4,3,0,2:T(8,128)(2,1)S(1)} %fusion.16) | data formatting | bytes 4194304
  263.9 6.5 %reshape.1664 = bf16[1024,1024]{1,0:T(8,128)(2,1)} reshape(bf16[8,128,1,16,64]{4,3,1,0,2:T(8,128)(2,1)} %copy.157) | data formatting | bytes 4194304
  (220 shorter events, 4.8 us)
Async XLA Ops:
  7.2 33.6 %copy-start = (bf16[1024,1,128]{2,0,1:T(8,128)(2,1)S(1)}, bf16[1024,1,128]{2,0,1:T(8,128)(2,1)}, u32[]{:S(2)}) copy-start(bf16[1024,1,128]{2,0,1:T(8,128)(2,1)} %param.11) | copy-start | bytes 786436
  7.2 98.7 %all-gather.5.cloned.1.call-start = ((), (), s32[]{:S(2)}) async-start(), calls=%async_computation | async-start | bytes 10027008 | tf_op jit(solution)/shard_map/all_gather | solution.py:107
  11.2 14.7 %copy-start.87 = (f32[16]{0:T(128)}, f32[16]{0:T(128)S(1)}, u32[]{:S(2)}) copy-start(f32[16]{0:T(128)S(1)} %get-tuple-element.45) | copy-start | bytes 196
  12.1 7.4 %copy-start.36 = (f32[8,128,16]{1,2,0:T(8,128)}, f32[8,128,16]{1,2,0:T(8,128)S(1)}, u32[]{:S(2)}) copy-start(f32[8,128,16]{1,2,0:T(8,128)S(1)} %get-tuple-element.88) | copy-start | bytes 196612
  19.7 2.7 copy-start.47
  19.7 2.7 copy-start.77
  19.7 2.7 copy-start.79
  19.7 2.7 copy-start.81
  19.7 2.7 copy-start.83
  19.7 2.7 copy-start.85
  19.8 17.3 %copy-start.45 = (f32[16]{0:T(128)}, f32[16]{0:T(128)S(1)}, u32[]{:S(2)}) copy-start(f32[16]{0:T(128)S(1)} %get-tuple-element.53) | copy-start | bytes 196
  24.3 2.9 %copy-start.7 = (bf16[1024,1024]{1,0:T(8,128)(2,1)S(1)}, bf16[1024,1024]{1,0:T(8,128)(2,1)}, u32[]{:S(2)}) copy-start(bf16[1024,1024]{1,0:T(8,128)(2,1)} %param.7) | copy-start | bytes 6291460
  25.9 12.4 %copy-start.17 = (f32[1,16,64,128]{3,2,1,0:T(8,128)}, f32[1,16,64,128]{3,2,1,0:T(8,128)S(1)}, u32[]{:S(2)}) copy-start(f32[1,16,64,128]{3,2,1,0:T(8,128)S(1)} %get-tuple-element.76) | copy-start | bytes 1572868
  27.0 194.2 %all-gather.7.cloned.1.call-start = ((), (), s32[]{:S(2)}) async-start(), calls=%async_computation.1 | async-start | bytes 8912896 | tf_op jit(solution)/shard_map/all_gather | solution.py:138
  37.0 3.6 %copy-start.21 = (f32[1,16,64,128]{3,2,1,0:T(8,128)S(1)}, f32[1,16,64,128]{3,2,1,0:T(8,128)}, u32[]{:S(2)}) copy-start(f32[1,16,64,128]{3,2,1,0:T(8,128)} %get-tuple-element.73) | copy-start | bytes 1572868
  37.0 3.7 %copy-start.23 = (f32[1,16,64,128]{3,2,1,0:T(8,128)S(1)}, f32[1,16,64,128]{3,2,1,0:T(8,128)}, u32[]{:S(2)}) copy-start(f32[1,16,64,128]{3,2,1,0:T(8,128)} %get-tuple-element.72) | copy-start | bytes 1572868
  37.0 3.8 %copy-start.28 = (bf16[1024,1,128]{2,0,1:T(8,128)(2,1)S(1)}, bf16[1024,1,128]{2,0,1:T(8,128)(2,1)}, u32[]{:S(2)}) copy-start(bf16[1024,1,128]{2,0,1:T(8,128)(2,1)} %param.10) | copy-start | bytes 786436
  37.0 5.8 %copy-start.42 = (pred[128,128]{1,0:T(8,128)(4,1)}, pred[128,128]{1,0:T(8,128)(4,1)S(1)}, u32[]{:S(2)}) copy-start(pred[128,128]{1,0:T(8,128)(4,1)S(1)} %iota_compare_fusion) | copy-start | bytes 49156
  41.1 3.8 %copy-start.30 = (bf16[8,128,16,64]{1,3,2,0:T(8,128)(2,1)S(1)}, bf16[8,128,16,64]{1,3,2,0:T(8,128)(2,1)}, u32[]{:S(2)}) copy-start(bf16[8,128,16,64]{1,3,2,0:T(8,128)(2,1)} %copy.112) | copy-start | bytes 6291460
  41.1 3.7 %copy-start.31 = (f32[8,128,16]{1,2,0:T(8,128)S(1)}, f32[8,128,16]{1,2,0:T(8,128)}, u32[]{:S(2)}) copy-start(f32[8,128,16]{1,2,0:T(8,128)} %get-tuple-element.87) | copy-start | bytes 196612
  61.5 44.3 %copy-start.90 = (pred[16]{0:T(512)(128)(4,1)}, pred[16]{0:T(512)(128)(4,1)S(1)}, u32[]{:S(2)}) copy-start(pred[16]{0:T(512)(128)(4,1)S(1)} %get-tuple-element.128) | copy-start | bytes 52
  110.0 4.0 %copy-start.26 = (f32[8,128,1,16,64]{1,4,3,0,2:T(8,128)S(1)}, f32[8,128,1,16,64]{1,4,3,0,2:T(8,128)}, u32[]{:S(2)}) copy-start(f32[8,128,1,16,64]{1,4,3,0,2:T(8,128)} %bitcast_add_fusion.1) | copy-start | bytes 12582916
  117.5 3.3 %copy-start.8 = (bf16[1024,1024]{0,1:T(8,128)(2,1)S(1)}, bf16[1024,1024]{0,1:T(8,128)(2,1)}, u32[]{:S(2)}) copy-start(bf16[1024,1024]{0,1:T(8,128)(2,1)} %copy.118) | copy-start | bytes 6291460
  117.5 3.3 %copy-start.9 = (bf16[1024,1024]{0,1:T(8,128)(2,1)S(1)}, bf16[1024,1024]{0,1:T(8,128)(2,1)}, u32[]{:S(2)}) copy-start(bf16[1024,1024]{0,1:T(8,128)(2,1)} %copy.119) | copy-start | bytes 6291460
  117.5 3.4 %copy-start.40 = (f32[1024]{0:T(1024)S(1)}, f32[1024]{0:T(1024)}, u32[]{:S(2)}) copy-start(f32[1024]{0:T(1024)} %param.12) | copy-start | bytes 12292
  120.8 3.4 %copy-start.3 = (f32[8,128,1,16,64]{1,0,4,3,2:T(8,128)}, f32[8,128,1,16,64]{1,0,4,3,2:T(8,128)S(1)}, u32[]{:S(2)}) copy-start(f32[8,128,1,16,64]{1,0,4,3,2:T(8,128)S(1)} %copy.117) | copy-start | bytes 12582916
  162.8 4.1 %copy-start.16 = (bf16[1024,1024]{0,1:T(8,128)(2,1)S(1)}, bf16[1024,1024]{0,1:T(8,128)(2,1)}, u32[]{:S(2)}) copy-start(bf16[1024,1024]{0,1:T(8,128)(2,1)} %get-tuple-element.83) | copy-start | bytes 6291460
  169.4 13.2 %copy-start.29 = (bf16[1024,1,128]{2,0,1:T(8,128)(2,1)S(1)}, bf16[1024,1,128]{2,0,1:T(8,128)(2,1)}, u32[]{:S(2)}) copy-start(bf16[1024,1,128]{2,0,1:T(8,128)(2,1)} %param.10) | copy-start | bytes 786436
  169.4 13.5 %copy-start.91 = (pred[16]{0:T(512)(128)(4,1)S(1)}, pred[16]{0:T(512)(128)(4,1)}, u32[]{:S(2)}) copy-start(pred[16]{0:T(512)(128)(4,1)} %copy-done.90) | copy-start | bytes 52
  169.4 13.7 %copy-start.2 = (f32[128,8,8,128]{3,2,1,0:T(8,128)S(1)}, f32[128,8,8,128]{3,2,1,0:T(8,128)}, u32[]{:S(2)}) copy-start(f32[128,8,8,128]{3,2,1,0:T(8,128)} %copy-done.1) | copy-start | bytes 12582916
  169.4 13.7 %copy-start.5 = (f32[8,1,16,64,128]{4,3,2,1,0:T(8,128)S(1)}, f32[8,1,16,64,128]{4,3,2,1,0:T(8,128)}, u32[]{:S(2)}) copy-start(f32[8,1,16,64,128]{4,3,2,1,0:T(8,128)} %copy-done.4) | copy-start | bytes 12582916
  169.4 13.7 %copy-start.32 = (f32[8,128,16]{1,2,0:T(8,128)S(1)}, f32[8,128,16]{1,2,0:T(8,128)}, u32[]{:S(2)}) copy-start(f32[8,128,16]{1,2,0:T(8,128)} %get-tuple-element.87) | copy-start | bytes 196612
  183.0 38.2 %copy-start.49 = (f32[16]{0:T(128)}, f32[16]{0:T(128)S(1)}, u32[]{:S(2)}) copy-start(f32[16]{0:T(128)S(1)} %get-tuple-element.92) | copy-start | bytes 196
  183.0 38.2 %copy-start.51 = (f32[16]{0:T(128)}, f32[16]{0:T(128)S(1)}, u32[]{:S(2)}) copy-start(f32[16]{0:T(128)S(1)} %get-tuple-element.93) | copy-start | bytes 196
  183.0 38.2 %copy-start.53 = (f32[16]{0:T(128)}, f32[16]{0:T(128)S(1)}, u32[]{:S(2)}) copy-start(f32[16]{0:T(128)S(1)} %get-tuple-element.94) | copy-start | bytes 196
  183.0 38.2 %copy-start.55 = (f32[16]{0:T(128)}, f32[16]{0:T(128)S(1)}, u32[]{:S(2)}) copy-start(f32[16]{0:T(128)S(1)} %get-tuple-element.95) | copy-start | bytes 196
  183.0 38.2 %copy-start.57 = (f32[16]{0:T(128)}, f32[16]{0:T(128)S(1)}, u32[]{:S(2)}) copy-start(f32[16]{0:T(128)S(1)} %get-tuple-element.96) | copy-start | bytes 196
  183.0 38.2 %copy-start.59 = (f32[16]{0:T(128)}, f32[16]{0:T(128)S(1)}, u32[]{:S(2)}) copy-start(f32[16]{0:T(128)S(1)} %get-tuple-element.97) | copy-start | bytes 196
  183.0 38.2 %copy-start.61 = (f32[16]{0:T(128)}, f32[16]{0:T(128)S(1)}, u32[]{:S(2)}) copy-start(f32[16]{0:T(128)S(1)} %get-tuple-element.98) | copy-start | bytes 196
  183.1 38.2 %copy-start.63 = (f32[16]{0:T(128)}, f32[16]{0:T(128)S(1)}, u32[]{:S(2)}) copy-start(f32[16]{0:T(128)S(1)} %get-tuple-element.99) | copy-start | bytes 196
  183.1 38.2 %copy-start.65 = (f32[16]{0:T(128)}, f32[16]{0:T(128)S(1)}, u32[]{:S(2)}) copy-start(f32[16]{0:T(128)S(1)} %get-tuple-element.100) | copy-start | bytes 196
  183.1 38.2 %copy-start.67 = (f32[16]{0:T(128)}, f32[16]{0:T(128)S(1)}, u32[]{:S(2)}) copy-start(f32[16]{0:T(128)S(1)} %get-tuple-element.101) | copy-start | bytes 196
  183.1 38.2 %copy-start.69 = (f32[16]{0:T(128)}, f32[16]{0:T(128)S(1)}, u32[]{:S(2)}) copy-start(f32[16]{0:T(128)S(1)} %get-tuple-element.102) | copy-start | bytes 196
  183.1 38.2 %copy-start.71 = (f32[16]{0:T(128)}, f32[16]{0:T(128)S(1)}, u32[]{:S(2)}) copy-start(f32[16]{0:T(128)S(1)} %get-tuple-element.103) | copy-start | bytes 196
  183.1 38.2 %copy-start.73 = (f32[16]{0:T(128)}, f32[16]{0:T(128)S(1)}, u32[]{:S(2)}) copy-start(f32[16]{0:T(128)S(1)} %get-tuple-element.104) | copy-start | bytes 196
  183.1 38.2 %copy-start.75 = (f32[16]{0:T(128)}, f32[16]{0:T(128)S(1)}, u32[]{:S(2)}) copy-start(f32[16]{0:T(128)S(1)} %get-tuple-element.105) | copy-start | bytes 196
  191.3 3.8 %copy-start.10 = (f32[16,64,8,128]{3,1,0,2:T(8,128)S(1)}, f32[16,64,8,128]{3,1,0,2:T(8,128)}, u32[]{:S(2)}) copy-start(f32[16,64,8,128]{3,1,0,2:T(8,128)} %get-tuple-element.125) | copy-start | bytes 12582916
  191.3 5.0 %copy-start.12 = (f32[8,16,64,128]{3,2,1,0:T(8,128)S(1)}, f32[8,16,64,128]{3,2,1,0:T(8,128)}, u32[]{:S(2)}) copy-start(f32[8,16,64,128]{3,2,1,0:T(8,128)} %copy-done.11) | copy-start | bytes 12582916
  221.3 4.7 %copy-start.15 = (f32[8,16,64,128]{3,2,1,0:T(8,128)S(1)}, f32[8,16,64,128]{3,2,1,0:T(8,128)}, u32[]{:S(2)}) copy-start(f32[8,16,64,128]{3,2,1,0:T(8,128)} %fusion.19) | copy-start | bytes 12582916
  221.3 4.8 %copy-start.24 = (f32[1,16,64,128]{3,2,1,0:T(8,128)S(1)}, f32[1,16,64,128]{3,2,1,0:T(8,128)}, u32[]{:S(2)}) copy-start(f32[1,16,64,128]{3,2,1,0:T(8,128)} %get-tuple-element.72) | copy-start | bytes 1572868
  221.3 4.7 %copy-start.86 = (f32[16]{0:T(128)S(1)}, f32[16]{0:T(128)}, u32[]{:S(2)}) copy-start(f32[16]{0:T(128)} %copy-done.85) | copy-start | bytes 196
  221.3 5.1 %copy-start.22 = (f32[1,16,64,128]{3,2,1,0:T(8,128)S(1)}, f32[1,16,64,128]{3,2,1,0:T(8,128)}, u32[]{:S(2)}) copy-start(f32[1,16,64,128]{3,2,1,0:T(8,128)} %get-tuple-element.73) | copy-start | bytes 1572868
  221.3 5.1 %copy-start.84 = (f32[16]{0:T(128)S(1)}, f32[16]{0:T(128)}, u32[]{:S(2)}) copy-start(f32[16]{0:T(128)} %copy-done.83) | copy-start | bytes 196
  221.3 9.0 %slice-start = ((s8[8388608]{0:T(1024)(128)(4,1)}), s8[4194304]{0:T(1024)(128)(4,1)S(1)}, s32[]{:S(2)}) async-start(s8[8388608]{0:T(1024)(128)(4,1)} %bitcast.599), calls=%async_computation.2 | async-start | bytes 8388608
  226.4 3.9 %slice-start.1 = ((s8[8388608]{0:T(1024)(128)(4,1)}), s8[4194304]{0:T(1024)(128)(4,1)S(1)}, s32[]{:S(2)}) async-start(s8[8388608]{0:T(1024)(128)(4,1)} %bitcast.599), calls=%async_computation.3 | async-start | bytes 8388608
  232.7 4.9 %copy-start.25 = (f32[8,128,1,16,64]{1,4,3,0,2:T(8,128)S(1)}, f32[8,128,1,16,64]{1,4,3,0,2:T(8,128)}, u32[]{:S(2)}) copy-start(f32[8,128,1,16,64]{1,4,3,0,2:T(8,128)} %copy.128) | copy-start | bytes 12582916
  237.6 3.7 %copy-start.88 = (f32[16]{0:T(128)S(1)}, f32[16]{0:T(128)}, u32[]{:S(2)}) copy-start(f32[16]{0:T(128)} %copy-done.87) | copy-start | bytes 196
  237.6 3.7 %copy-start.92 = (f32[16]{0:T(128)S(1)}, f32[16]{0:T(128)}, u32[]{:S(2)}) copy-start(f32[16]{0:T(128)} %get-tuple-element.37) | copy-start | bytes 196
  237.6 3.7 %copy-start.41 = (f32[8,16]{1,0:T(8,128)S(1)}, f32[8,16]{1,0:T(8,128)}, u32[]{:S(2)}) copy-start(f32[8,16]{1,0:T(8,128)} %get-tuple-element.43) | copy-start | bytes 1540
  237.6 3.7 %copy-start.89 = (f32[16]{0:T(128)S(1)}, f32[16]{0:T(128)}, u32[]{:S(2)}) copy-start(f32[16]{0:T(128)} %get-tuple-element.38) | copy-start | bytes 196
  237.6 3.9 %copy-start.35 = (f32[8,128,16]{1,2,0:T(8,128)S(1)}, f32[8,128,16]{1,2,0:T(8,128)}, u32[]{:S(2)}) copy-start(f32[8,128,16]{1,2,0:T(8,128)} %get-tuple-element.36) | copy-start | bytes 196612
  237.6 3.9 %copy-start.38 = (f32[8,16,128]{2,1,0:T(8,128)S(1)}, f32[8,16,128]{2,1,0:T(8,128)}, u32[]{:S(2)}) copy-start(f32[8,16,128]{2,1,0:T(8,128)} %get-tuple-element.30) | copy-start | bytes 196612
  237.6 3.8 %copy-start.39 = (f32[8,16,128]{2,1,0:T(8,128)S(1)}, f32[8,16,128]{2,1,0:T(8,128)}, u32[]{:S(2)}) copy-start(f32[8,16,128]{2,1,0:T(8,128)} %get-tuple-element.31) | copy-start | bytes 196612
  237.6 14.6 %copy-start.37 = (f32[8,128,16]{1,2,0:T(8,128)S(1)}, f32[8,128,16]{1,2,0:T(8,128)}, u32[]{:S(2)}) copy-start(f32[8,128,16]{1,2,0:T(8,128)} %copy-done.36) | copy-start | bytes 196612
  (33 other events, 71.6 us)
Sparse Core Ops, SparseCore 0:
  27.1 78.7 all-gather.4
  151.2 69.9 all-gather.6
where the time goes:
time: 282 us; the launch traced here: 278 us
  local copies, waits for them, and re-layouts  74 us (26%)
  waiting for transfers between devices  66 us (23%)
  matrix products  58 us (21%)
  other arithmetic  49.7 us (18%)
  between operations  15.6 us (6%)
  blocking collectives  13.9 us (5%)
    all_gather x1, waiting for transfers between devices, device_body(): packed = lax.all_gather(jnp.concatenate([final, log_rows], axis=2), 'seq')  44.3 us
    unnamed x206, local copies, waits for them, and re-layouts  44.1 us
    dot_general x3, matrix products, span_core(): jnp.einsum('kgrij,kjgrp->kigrp', weighted, x_blocks, precision=PRECISION)  28.8 us
    all_gather x1, waiting for transfers between devices, device_body(): gathered_leaving = lax.all_gather(leaving, 'seq')  21.7 us
    psum x1, blocking collectives, device_body(): lax.psum((jnp.sum(gated * gated, axis=1), jnp.sum(gated * scaled_cot, axi...  13.9 us
    another operation x2, other arithmetic, span_core(): running = jnp.cumsum(jnp.moveaxis(a_blocks, 1, 3), axis=3)  12.2 us
    reshape x2, local copies, waits for them, and re-layouts, device_body(): inputs.astype(jnp.float32)  11.7 us
    another operation x2, local copies, waits for them, and re-layouts  9.81 us
  transfers between devices with their start and end apart: 2, of which 2 were waited for; matrix products, arithmetic and copies ran while one was open for 28% of the time, Pallas kernels for 0%

commit v1 on v0

--- a/solution.py
+++ b/solution.py
@@ -42,8 +42,23 @@
     return (grad_b, grad_c)
 
 
-def span_core(x_blocks, a_blocks, b_blocks, c_blocks, scores):
+def block_chain(x_blocks, a_blocks, b_blocks):
     running = jnp.cumsum(jnp.moveaxis(a_blocks, 1, 3), axis=3)
+    span_end = running[..., -1]
+    to_end = jnp.exp(span_end[..., None] - running)
+    scaled = x_blocks * jnp.moveaxis(to_end, 3, 1)[..., None]
+    block_states = jnp.einsum("kjgrp,kjgn->kgrpn", scaled, b_blocks, precision=PRECISION)
+    factors = jnp.exp(span_end)
+    carried = jnp.zeros(block_states.shape[1:], jnp.float32)
+    start_list = []
+    for block in range(block_states.shape[0]):
+        start_list.append(carried)
+        carried = factors[block][..., None, None] * carried + block_states[block]
+    return (running, span_end, jnp.stack(start_list), carried)
+
+
+def local_core(x_blocks, a_blocks, b_blocks, c_blocks, scores):
+    running, span_end, starts, _ = block_chain(x_blocks, a_blocks, b_blocks)
     length = running.shape[3]
     row_numbers = lax.broadcasted_iota(jnp.int32, (length, length), 0)
     col_ids = lax.broadcasted_iota(jnp.int32, (length, length), 1)
@@ -52,36 +67,34 @@
     decays = jnp.exp(jnp.where(causal, log_gaps, -1e30))
     weighted = decays * scores[:, :, None]
     diagonal = jnp.einsum("kgrij,kjgrp->kigrp", weighted, x_blocks, precision=PRECISION)
-    span_end = running[..., -1]
-    to_end = jnp.exp(span_end[..., None] - running)
-    scaled = x_blocks * jnp.moveaxis(to_end, 3, 1)[..., None]
-    block_states = jnp.einsum("kjgrp,kjgn->kgrpn", scaled, b_blocks, precision=PRECISION)
-
-    factors = jnp.exp(span_end)
-    carried = jnp.zeros(block_states.shape[1:], jnp.float32)
-    start_list = []
-    for block in range(block_states.shape[0]):
-        start_list.append(carried)
-        carried = factors[block][..., None, None] * carried + block_states[block]
-    final = carried
-    starts = jnp.stack(start_list)
     from_state = jnp.einsum("kign,kgrpn->kigrp", c_blocks, starts, precision=PRECISION)
-    ssd_out = diagonal + from_state * jnp.moveaxis(jnp.exp(running), 3, 1)[..., None]
-    return (ssd_out, final, running, span_end)
-
-
-def local_core(x_blocks, a_blocks, b_blocks, c_blocks, scores):
-    ssd_part, final, running, span_end = span_core(x_blocks, a_blocks, b_blocks, c_blocks, scores)
+    ssd_part = diagonal + from_state * jnp.moveaxis(jnp.exp(running), 3, 1)[..., None]
     earlier = jnp.cumsum(span_end, axis=0) - span_end
     reach = jnp.exp(running + earlier[..., None])
-    log_carry = jnp.sum(span_end, axis=0)
-    return (ssd_part, final, reach, jnp.exp(log_carry), log_carry)
-
-
-def add_incoming(ssd_part, final, reach, carry_all, c_blocks, incoming):
+    return (ssd_part, reach)
+
+
+def edge_grads(adjoint, carry_grad, x_blocks, b_blocks, to_end, later, carry_all):
+    tokens = x_blocks.shape[0] * x_blocks.shape[1]
+    x_tok = x_blocks.reshape((tokens,) + x_blocks.shape[2:])
+    b_tok = b_blocks.reshape((tokens,) + b_blocks.shape[2:])
+    weights = jnp.exp(jnp.moveaxis(to_end + later[..., None], 3, 1))
+    weights = weights.reshape((tokens,) + weights.shape[2:])
+    projected = jnp.einsum("tgn,grpn->tgrp", b_tok, adjoint, precision=PRECISION)
+    grad_x = weights[..., None] * projected
+    log_grad = weights * jnp.sum(x_tok * projected, axis=3)
+    grad_b = jnp.einsum("tgrp,grpn->tgn", weights[..., None] * x_tok, adjoint, precision=PRECISION)
+    grad_a = jnp.cumsum(log_grad, axis=0) - log_grad + (carry_grad * carry_all)[None]
+    return (
+        grad_x.reshape(x_blocks.shape),
+        grad_a.reshape(x_blocks.shape[:4]),
+        grad_b.reshape(b_blocks.shape),
+    )
+
+
+def add_incoming(ssd_part, reach, c_blocks, incoming):
     projected = jnp.einsum("kign,grpn->kigrp", c_blocks, incoming, precision=PRECISION)
-    from_left = projected * jnp.moveaxis(reach, 3, 1)[..., None]
-    return (ssd_part + from_left, carry_all[..., None, None] * incoming + final)
+    return ssd_part + projected * jnp.moveaxis(reach, 3, 1)[..., None]
 
 
 def device_body(inputs, gate_input, log_decay, b_matrix, c_matrix, norm_gain, cotangent):
@@ -101,24 +114,29 @@
     c_blocks = c_half.astype(jnp.float32)
     scores = pair_scores(c_half, b_half)
     core_out, core_pull = jax.vjp(local_core, x_blocks, a_blocks, b_blocks, c_blocks, scores)
-    ssd_part, final, reach, carry_all, log_carry = core_out
+    ssd_part, reach = core_out
     ssd_part = lax.optimization_barrier(ssd_part)
+    running, span_end, _, final = block_chain(x_blocks, a_blocks, b_blocks)
+    carry_all = jnp.exp(jnp.sum(span_end, axis=0))
+    to_end = span_end[..., None] - running
+    later = jnp.cumsum(span_end[::-1], axis=0)[::-1] - span_end
+    log_carry = jnp.sum(a_blocks, axis=(0, 1))
     log_rows = jnp.broadcast_to(log_carry[..., None, None], final.shape[:2] + (8, final.shape[3]))
     packed = lax.all_gather(jnp.concatenate([final, log_rows], axis=2), "seq")
     head_size_p = final.shape[2]
     gathered_log = jnp.max(packed[:, :, :, head_size_p:], axis=(3, 4))
     incoming = weighted_sum(shard_weights(gathered_log, False), packed)[:, :, :head_size_p]
 
-    def light_step(part_a, part_b, part_c, part_d, part_e):
-        return add_incoming(part_a, part_b, part_c, part_d, part_e, incoming)
-
-    light_out, light_pull = jax.vjp(light_step, ssd_part, final, reach, carry_all, c_blocks)
-    ssd_out = light_out[0].reshape(tok_rows, width)
+    def light_step(part_a, part_b, part_c):
+        return add_incoming(part_a, part_b, part_c, incoming)
+
+    light_out, light_pull = jax.vjp(light_step, ssd_part, reach, c_blocks)
+    ssd_out = light_out.reshape(tok_rows, width)
     gate_value = gate_input.astype(jnp.float32)
     sigmoid_gate = jax.nn.sigmoid(gate_value)
     gate_silu = gate_value * sigmoid_gate
+    scaled_cot = norm_gain[None, :] * cotangent.astype(jnp.float32)
     gated = ssd_out * gate_silu
-    scaled_cot = norm_gain[None, :] * cotangent.astype(jnp.float32)
     squares, products = lax.psum(
         (jnp.sum(gated * gated, axis=1), jnp.sum(gated * scaled_cot, axis=1)), "head"
     )
@@ -137,13 +155,18 @@
     leaving = jnp.einsum("kign,kigrp->grpn", c_blocks, reached, precision=PRECISION)
     gathered_leaving = lax.all_gather(leaving, "seq")
     adjoint = weighted_sum(shard_weights(gathered_log, True), gathered_leaving)
-    light_grads = light_pull((upstream, adjoint))
-    grad_x, grad_a, grad_b_core, grad_c_core, grad_scores = core_pull(
-        tuple(light_grads[:4]) + (jnp.zeros_like(log_carry),)
-    )
+    light_grads = light_pull(upstream)
+    core_grads = lax.optimization_barrier(core_pull(tuple(light_grads[:2])))
+    carry_grad = jnp.sum(adjoint * incoming, axis=(2, 3))
+    edge_x, edge_a, edge_b = edge_grads(
+        adjoint, carry_grad, x_blocks, b_blocks, to_end, later, carry_all
+    )
+    grad_x_core, grad_a_core, grad_b_core, grad_c_core, grad_scores = core_grads
     extra_b, extra_c = score_grads(grad_scores, b_blocks, c_blocks)
-    grad_b = grad_b_core + extra_b
-    grad_c = grad_c_core + extra_c + light_grads[4]
+    grad_x = grad_x_core + edge_x
+    grad_a = grad_a_core + edge_a
+    grad_b = grad_b_core + extra_b + edge_b
+    grad_c = grad_c_core + extra_c + light_grads[2]
     grad_inputs = grad_x.reshape(tok_rows, width).astype(jnp.bfloat16)
     grad_decay = grad_a.reshape(tok_rows, head_count)
     grad_b_matrix = grad_b.reshape(tok_rows, groups, state_size)

time: 282 us -> 289 us (1.025)
  the two profiles are of different devices: /device:TPU:1 before, /device:TPU:0 now
where the time goes in v1:
time: 289 us; the launch traced here: 284 us
  matrix products  81 us (28%)
  other arithmetic  66.5 us (23%)
  waiting for transfers between devices  54.3 us (19%)
  local copies, waits for them, and re-layouts  51 us (18%)
  blocking collectives  15.6 us (5%)
  between operations  15.6 us (5%)
    all_gather x1, waiting for transfers between devices, device_body(): packed = lax.all_gather(jnp.concatenate([final, log_rows], axis=2), 'seq')  54.2 us
    unnamed x210, local copies, waits for them, and re-layouts  43.7 us
    dot_general x3, matrix products, local_core(): jnp.einsum('kgrij,kjgrp->kigrp', weighted, x_blocks, precision=PRECISION)  28.1 us
    psum x1, blocking collectives, device_body(): lax.psum((jnp.sum(gated * gated, axis=1), jnp.sum(gated * scaled_cot, axi...  15.6 us
    dot_general x3, matrix products, local_core(): jnp.einsum('kign,kgrpn->kigrp', c_blocks, starts, precision=PRECISION)  13.5 us
    another operation x2, other arithmetic, block_chain(): running = jnp.cumsum(jnp.moveaxis(a_blocks, 1, 3), axis=3)  12.2 us
    dot_general x2, matrix products, add_incoming(): jnp.einsum('kign,grpn->kigrp', c_blocks, incoming, precision=PRECISION)  10 us
    dot_general x3, matrix products, block_chain(): jnp.einsum('kjgrp,kjgn->kgrpn', scaled, b_blocks, precision=PRECISION)  9.53 us
  transfers between devices with their start and end apart: 2, of which 1 were waited for; matrix products, arithmetic and copies ran while one was open for 34% of the time, Pallas kernels for 0%

profile of v1, /device:TPU:0, one launch (start us, length us, event | category | flops | bytes accessed | tf_op | source)
XLA Modules:
  0.0 284.2 jit_solution(9493389376426103939)
XLA Ops:
  7.2 0.9 copy.193
  8.1 2.3 reduce_window_sum.73
  10.4 0.7 slice_reduce_fusion.1
  11.3 1.5 reduce_sum.209
  13.5 2.9 %copy.134 = bf16[1024,1024]{0,1:T(8,128)(2,1)S(1)} copy(bf16[1024,1024]{1,0:T(8,128)(2,1)} %param.7) | data formatting | bytes 4194304 | tf_op args[0]
  16.4 2.7 fusion.280
  19.1 3.0 %copy.194 = f32[128,8,8,128]{3,2,1,0:T(8,128)} copy(f32[128,8,8,128]{3,1,2,0:T(8,128)S(1)} %get-tuple-element.87) | data formatting | bytes 8388608
  22.9 2.6 broadcast_multiply_fusion.1
  25.5 1.6 fusion.52
  27.6 1.9 copy-done.5
  29.5 1.4 slice_add_fusion.7
  31.0 0.9 pad_maximum_fusion
  32.9 1.7 bitcast_dynamic-update-slice_fusion.6
  35.2 1.3 bitcast_dynamic-update-slice_fusion
  36.6 1.4 fusion.30
  38.0 0.7 copy-done.6
  38.7 2.0 copy-done.9
  40.7 7.8 %bitcast_add_fusion.1 = f32[8,128,1,16,64]{1,4,3,0,2:T(8,128)} fusion(f32[8,16,64,128]{3,2,1,0:T(8,128)S(1)} %fusion.30, f32[8,128,16]{1,2,0:T(8,128)S(1)} %copy-done.42, f32[8,128,128]{2,1,0:T(8,128)S(1)} %fusion.282, f32[8,16,128]{2,1,0:T(8,128)S(1)} %bitcast.735, pred[128,128]{1,0:T(8,128)(4,1)S(1)} %iota_compare_fusion, ...), kind=kOutput, calls=%fused_computation.23 | convolution fusion | flops 813694976 | bytes 11157504 | tf_op jit(solution)/shard_map/jvp(kgrij,kjgrp->kigrp)/dot_general | solution.py:69
  48.5 2.9 %copy.141 = bf16[1024,1024]{0,1:T(8,128)(2,1)S(1)} copy(bf16[1024,1024]{1,0:T(8,128)(2,1)} %param.8) | data formatting | bytes 4194304 | tf_op args[1]
  51.4 4.0 %copy.142 = bf16[1024,1024]{0,1:T(8,128)(2,1)} copy(bf16[1024,1024]{1,0:T(8,128)(2,1)} %param.13) | data formatting | bytes 4194304 | tf_op args[6]
  55.3 0.7 copy.160
  56.0 54.2 %all-gather.5.cloned.1.call-done = f32[16,16,72,128]{3,2,1,0:T(8,128)} async-done(((f32[1,16,72,128]{3,2,1,0:T(8,128)}), f32[16,16,72,128]{3,2,1,0:T(8,128)}) %all-gather.5.cloned.1.call-update) | async-done | bytes 9437200 | tf_op jit(solution)/shard_map/all_gather | solution.py:125
  110.3 1.7 slice_reduce_fusion
  111.9 0.7 select_reduce_fusion
  112.7 2.2 slice_multiply_fusion
  114.9 3.3 %fusion.96 = f32[1,16,72,128]{3,2,1,0:T(8,128)S(1)} fusion(f32[16,16,72,128]{3,2,1,0:T(8,128)} %all-gather.5.cloned.1.call-done, f32[16]{0:T(128)S(1)} %get-tuple-element.114, f32[16]{0:T(128)S(1)} %get-tuple-element.115, f32[16]{0:T(128)S(1)} %get-tuple-element.116, f32[16]{0:T(128)S(1)} %get-tuple-element.117, f32[16]{0:T(128)S(1)} %get-tuple-element.118, ...), kind=kLoop, calls=%fused_computation.107 | loop fusion | flops 2801664 | bytes 6488704 | tf_op jit(solution)/shard_map/add | solution.py:31
  118.9 3.6 %fusion.23 = (f32[8,128,1,16,64]{1,4,3,0,2:T(8,128)S(1)}, f32[16,64,8,128]{3,1,0,2:T(8,128)}) fusion(f32[8,128,1,16,64]{1,4,3,0,2:T(8,128)S(1)} %copy-done.24, f32[8,128,16]{1,2,0:T(8,128)S(1)} %get-tuple-element.89, bf16[8,128,128,1]{2,1,3,0:T(8,128)(2,1)S(1)} %bitcast.709, f32[1,16,64,128]{3,2,1,0:T(8,128)S(1)} %fusion.105), kind=kOutput, calls=%fused_computation.39 | convolution fusion | flops 807403520 | bytes 13434880 | tf_op jit(solution)/shard_map/jvp(kign,grpn->kigrp)/dot_general | solution.py:96
  122.5 3.3 %copy.140 = f32[8,128,1,16,64]{1,0,4,3,2:T(8,128)S(1)} copy(f32[8,128,1,16,64]{1,4,3,0,2:T(8,128)S(1)} %get-tuple-element.136) | data formatting | bytes 8388608 | tf_op jit(solution)/shard_map/jvp()/add | solution.py:97
  125.8 3.4 %multiply_reduce_fusion.1 = (f32[1024]{0:T(1024)S(1)}, f32[1024]{0:T(1024)}) fusion(bf16[1024,1024]{0,1:T(8,128)(2,1)S(1)} %copy-done.7, f32[1024]{0:T(1024)S(1)} %copy-done.60, bf16[1024,1024]{0,1:T(8,128)(2,1)S(1)} %copy.141, f32[128,8,8,128]{3,2,1,0:T(8,128)S(1)} %bitcast.721), kind=kLoop, calls=%fused_computation.58 | loop fusion | flops 12580864 | bytes 8400896 | tf_op jit(solution)/shard_map/reduce_sum | solution.py:141
  129.2 15.6 %all-reduce.15 = (f32[1024]{0:T(1024)}, f32[1024]{0:T(1024)}) all-reduce(f32[1024]{0:T(1024)} %get-tuple-element.44, f32[1024]{0:T(1024)S(1)} %get-tuple-element.43), channel_id=1, replica_groups=mesh['seq'=16,'head'=8] {'head'}, use_global_device_ids=true, to_apply=%region_6.7 | all-reduce | flops 2048 | bytes 16384 | tf_op jit(solution)/shard_map/psum | solution.py:140
  144.8 0.7 fusion.274
  145.5 6.9 %fusion.12 = (bf16[1024,1024]{0,1:T(8,128)(2,1)}, f32[128,8,8,128]{3,1,2,0:T(8,128)S(1)}, bf16[1024,1024]{0,1:T(8,128)(2,1)}) fusion(bf16[1024,1024]{0,1:T(8,128)(2,1)S(1)} %copy.141, f32[128,8,8,128]{3,2,1,0:T(8,128)} %bitcast.722, bf16[1024,1024]{0,1:T(8,128)(2,1)} %copy.142, f32[1024]{0:T(1024)S(1)} %get-tuple-element.126, f32[1024]{0:T(1024)S(1)} %copy-done.60, ...), kind=kLoop, calls=%fused_computation.16 | loop fusion | flops 23068672 | bytes 16789504 | tf_op jit(solution)/shard_map/convert_element_type | solution.py:151
  152.4 1.0 copy.197
  153.8 1.6 copy-done.1
  155.4 2.1 fusion.71
  157.6 3.9 %fusion.19 = f32[8,16,64,128]{3,2,1,0:T(8,128)S(1)} fusion(bf16[8,128,128,1]{2,1,3,0:T(8,128)(2,1)S(1)} %bitcast.710, f32[8,128,1,16,64]{1,0,4,3,2:T(8,128)} %bitcast.715, f32[8,128,16]{1,2,0:T(8,128)S(1)} %copy-done.43), kind=kOutput, calls=%fused_computation.29 | convolution fusion | flops 806354944 | bytes 8716288 | tf_op jit(solution)/shard_map/transpose(jvp(kign,kgrpn->kigrp))/dot_general | solution.py:70
  161.5 0.9 multiply_reduce_fusion.8
  162.4 0.8 multiply_reduce_fusion.7
  163.3 0.8 multiply_reduce_fusion.6
  164.1 0.9 multiply_reduce_fusion.5
  165.0 3.1 %multiply_reduce_fusion.9 = (f32[16]{0:T(128)}, f32[16]{0:T(128)}, f32[16]{0:T(128)}, f32[1,16,64,128]{3,2,1,0:T(8,128)S(1)}) fusion(f32[1,16,64,128]{3,2,1,0:T(8,128)S(1)} %get-tuple-element.68, f32[8,16,64,128]{3,2,1,0:T(8,128)S(1)} %fusion.19, f32[16]{0:T(128)S(1)} %copy-done.69, f32[8,16,64,128]{3,2,1,0:T(8,128)} %copy-done.5, f32[16]{0:T(128)S(1)} %copy-done.67, ...), kind=kLoop, calls=%fused_computation.266 | loop fusion | flops 1441744 | bytes 3670400 | tf_op jit(solution)/shard_map/transpose(jvp())/reduce_sum | solution.py:56
  168.6 2.3 fusion.24
  171.1 3.6 %fusion.21 = (f32[8,128,16]{1,2,0:T(8,128)S(1)}, f32[8,16,64,128]{3,2,1,0:T(8,128)}) fusion(f32[8,128,1,16,64]{1,0,4,3,2:T(8,128)S(1)} %bitcast.725, bf16[8,128,128,1]{2,1,3,0:T(8,128)(2,1)S(1)} %bitcast.733, f32[1,1,16,64,128]{4,3,2,1,0:T(8,128)S(1)} %get-tuple-element.85, f32[1,1,16,64,128]{4,3,2,1,0:T(8,128)S(1)} %bitcast.751, ...), kind=kOutput, calls=%fused_computation.33 | convolution fusion | flops 813678592 | bytes 12386304 | tf_op jit(solution)/shard_map/transpose(jvp(kjgrp,kjgn->kgrpn))/dot_general | solution.py:50
  176.0 0.7 fusion.275
  176.7 0.8 copy.157
  177.4 12.8 %fusion.6 = (f32[8,16,128]{2,1,0:T(8,128)S(1)}, f32[8,16,128]{2,1,0:T(8,128)S(1)}, f32[8,128,128]{2,1,0:T(8,128)}) fusion(f32[8,128,128]{2,1,0:T(8,128)} %copy-done.45, f32[8,16,128]{2,1,0:T(8,128)S(1)} %bitcast.736, pred[128,128]{1,0:T(8,128)(4,1)} %copy-done.62, bf16[8,128,16,64]{1,0,3,2:T(8,128)(2,1)S(1)} %bitcast.739, f32[8,16,64,128]{3,0,2,1:T(8,128)} %bitcast.716), kind=kOutput, calls=%fused_computation.10 | convolution fusion | flops 824016896 | bytes 7553024 | tf_op jit(solution)/shard_map/transpose(jvp(kgrij,kjgrp->kigrp))/dot_general | solution.py:69
  190.4 9.9 %reduce_window_sum.76 = f32[8,1,16,128]{3,2,1,0:T(8,128)S(1)} reduce-window(f32[8,1,16,128]{3,2,1,0:T(8,128)S(1)} %fusion.264, f32[]{:T(128)} %constant.35.clone.1), window={size=1x1x1x128 pad=0_0x0_0x0_0x0_127}, to_apply=%region_24.25 | reduce-window | flops 2080768 | bytes 131076 | tf_op jit(solution)/shard_map/transpose(jvp(jit(cumsum)))/reduce_window_sum | solution.py:46
  200.4 8.3 %fusion.79 = f32[8,128,1,128]{3,1,0,2:T(8,128)} fusion(f32[8,1,16,64,128]{4,3,2,1,0:T(8,128)} %copy-done.6, f32[8,128,1,16,64]{1,0,4,3,2:T(8,128)} %bitcast.717, f32[8,128,16]{1,2,0:T(8,128)S(1)} %copy-done.44), kind=kOutput, calls=%fused_computation.93 | convolution fusion | flops 806354944 | bytes 8978432 | tf_op jit(solution)/shard_map/transpose(jvp(kign,kgrpn->kigrp))/dot_general | solution.py:70
  208.8 4.3 %fusion.74 = f32[8,128,1,128]{1,3,0,2:T(8,128)} fusion(f32[8,128,16,64]{1,0,3,2:T(8,128)S(1)} %copy-done.12, f32[1,1,16,64,128]{4,3,2,1,0:T(8,128)S(1)} %copy-done.50, f32[1,1,16,64,128]{4,3,2,1,0:T(8,128)S(1)} %bitcast.752, f32[1,1,16,64,128]{4,3,2,1,0:T(8,128)S(1)} %bitcast.750, f32[1,1,16,64,128]{4,3,2,1,0:T(8,128)S(1)} %bitcast.748, ...), kind=kOutput, calls=%fused_computation.92 | convolution fusion | flops 811597824 | bytes 8388608 | tf_op jit(solution)/shard_map/transpose(jvp(kjgrp,kjgn->kgrpn))/dot_general | solution.py:50
  213.1 7.5 %bitcast_add_fusion = f32[8,128,1,16,64]{1,4,3,0,2:T(8,128)} fusion(f32[8,16,64,128]{3,2,1,0:T(8,128)S(1)} %copy-done.94, f32[8,128,16]{1,2,0:T(8,128)S(1)} %copy-done.55, f32[8,128,128]{2,1,0:T(8,128)S(1)} %copy-done.46, f32[8,16,128]{2,1,0:T(8,128)S(1)} %bitcast.737, pred[128,128]{1,0:T(8,128)(4,1)S(1)} %copy-done.63, f32[8,16,64,128]{3,0,2,1:T(8,128)S(1)} %bitcast.720), kind=kOutput, calls=%fused_computation.22 | convolution fusion | flops 813694976 | bytes 13254656 | tf_op jit(solution)/shard_map/transpose(jvp(kgrij,kjgrp->kigrp))/dot_general | solution.py:69
  220.7 4.1 %copy.177 = bf16[1024,1024]{1,0:T(8,128)(2,1)} copy(bf16[1024,1024]{0,1:T(8,128)(2,1)} %get-tuple-element.81) | data formatting | bytes 4194304
  224.8 2.5 copy.179
  227.5 1.5 fusion.95
  229.1 6.4 %fusion.90 = f32[8,128,1,128]{3,1,0,2:T(8,128)} fusion(f32[8,128,1,128]{3,1,0,2:T(8,128)S(1)} %fusion.95, f32[8,128,1,16,64]{1,0,4,3,2:T(8,128)} %bitcast.718, f32[8,128,16]{1,2,0:T(8,128)S(1)} %get-tuple-element.89, f32[1,16,64,128]{3,2,1,0:T(8,128)S(1)} %fusion.105), kind=kOutput, calls=%fused_computation.98 | convolution fusion | flops 806486016 | bytes 5832704 | tf_op jit(solution)/shard_map/transpose(jvp(kign,grpn->kigrp))/dot_general | solution.py:96
  235.5 6.7 %fusion.84 = f32[1024,1,128]{0,2,1:T(8,128)S(1)} fusion(f32[1024,16,64]{0,2,1:T(8,128)} %bitcast.727, f32[1024,16]{0,1:T(8,128)S(1)} %bitcast.757, f32[256,64,128]{2,1,0:T(8,128)} %all-gather.7.cloned.1.call-done, f32[16]{0:T(128)S(1)} %get-tuple-element.93, f32[16]{0:T(128)S(1)} %get-tuple-element.94, f32[16]{0:T(128)S(1)} %get-tuple-element.95, ...), kind=kOutput, calls=%fused_computation.96 | convolution fusion | flops 810418176 | bytes 13173760 | tf_op jit(solution)/shard_map/tgrp,grpn->tgn/dot_general | solution.py:86
  243.1 1.0 copy.175
  244.1 8.8 %fusion.16 = (f32[1024,16]{0,1:T(8,128)S(1)}, f32[1024,1,16,64]{0,3,2,1:T(8,128)}) fusion(f32[1024,1,16,64]{0,3,2,1:T(8,128)} %bitcast.728, f32[1024,16]{0,1:T(8,128)S(1)} %bitcast.758, bf16[1024,1,128]{2,0,1:T(8,128)(2,1)S(1)} %copy-done.28, f32[256,64,128]{2,1,0:T(8,128)} %all-gather.7.cloned.1.call-done, f32[16]{0:T(128)S(1)} %get-tuple-element.93, ...), kind=kOutput, calls=%fused_computation.26 | convolution fusion | flops 812498944 | bytes 17171456 | tf_op jit(solution)/shard_map/tgn,grpn->tgrp/dot_general | solution.py:83
  253.0 4.5 %reduce-window.6 = f32[16,1,8,128]{3,2,1,0:T(8,128)S(1)} reduce-window(f32[16,1,8,128]{3,2,1,0:T(8,128)S(1)} %bitcast.753, f32[]{:T(128)} %constant.35.clone.1), window={size=1x1x1x128 pad=0_0x0_0x0_0x127_0}, to_apply=%region_29.30 | reduce-window | flops 2080768 | bytes 131076 | tf_op jit(solution)/shard_map/reduce-window
  257.9 4.3 %fusion.114 = f32[16]{0:T(128)S(1)} fusion(f32[1,16,64,128]{3,2,1,0:T(8,128)S(1)} %fusion.105, f32[256,64,128]{2,1,0:T(8,128)} %all-gather.7.cloned.1.call-done, f32[16]{0:T(128)S(1)} %get-tuple-element.93, f32[16]{0:T(128)S(1)} %get-tuple-element.94, f32[16]{0:T(128)S(1)} %get-tuple-element.95, f32[16]{0:T(128)} %copy-done.78, f32[16]{0:T(128)} %copy-done.79, ...), kind=kLoop, calls=%fused_computation.156 | loop fusion | flops 4325360 | bytes 8913984 | tf_op jit(solution)/shard_map/reduce_sum | solution.py:160
  263.1 1.0 copy.201
  264.2 1.1 copy-done.25
  265.3 1.1 fusion.32
  266.4 4.2 %copy.191 = bf16[8,128,1,16,64]{4,3,1,0,2:T(8,128)(2,1)} copy(bf16[8,128,1,16,64]{1,4,3,0,2:T(8,128)(2,1)S(1)} %fusion.32) | data formatting | bytes 4194304
  270.6 6.5 %reshape.1448 = bf16[1024,1024]{1,0:T(8,128)(2,1)} reshape(bf16[8,128,1,16,64]{4,3,1,0,2:T(8,128)(2,1)} %copy.191) | data formatting | bytes 4194304
  (240 shorter events, 9.0 us)
Async XLA Ops:
  7.2 27.7 %copy-start = (bf16[1024,1,128]{2,0,1:T(8,128)(2,1)S(1)}, bf16[1024,1,128]{2,0,1:T(8,128)(2,1)}, u32[]{:S(2)}) copy-start(bf16[1024,1,128]{2,0,1:T(8,128)(2,1)} %param.11) | copy-start | bytes 786436
  7.2 103.1 %all-gather.5.cloned.1.call-start = ((), (), s32[]{:S(2)}) async-start(), calls=%async_computation | async-start | bytes 10027008 | tf_op jit(solution)/shard_map/all_gather | solution.py:125
  13.5 5.7 %copy-start.54 = (f32[8,128,16]{1,2,0:T(8,128)}, f32[8,128,16]{1,2,0:T(8,128)S(1)}, u32[]{:S(2)}) copy-start(f32[8,128,16]{1,2,0:T(8,128)S(1)} %get-tuple-element.91) | copy-start | bytes 196612
  22.8 4.7 %copy-start.68 = (f32[16]{0:T(128)}, f32[16]{0:T(128)S(1)}, u32[]{:S(2)}) copy-start(f32[16]{0:T(128)S(1)} %get-tuple-element.128) | copy-start | bytes 196
  22.8 4.7 %copy-start.70 = (f32[16]{0:T(128)}, f32[16]{0:T(128)S(1)}, u32[]{:S(2)}) copy-start(f32[16]{0:T(128)S(1)} %get-tuple-element.133) | copy-start | bytes 196
  22.8 4.7 %copy-start.72 = (f32[16]{0:T(128)}, f32[16]{0:T(128)S(1)}, u32[]{:S(2)}) copy-start(f32[16]{0:T(128)S(1)} %get-tuple-element.132) | copy-start | bytes 196
  22.8 4.7 %copy-start.74 = (f32[16]{0:T(128)}, f32[16]{0:T(128)S(1)}, u32[]{:S(2)}) copy-start(f32[16]{0:T(128)S(1)} %get-tuple-element.131) | copy-start | bytes 196
  22.9 4.7 %copy-start.76 = (f32[16]{0:T(128)}, f32[16]{0:T(128)S(1)}, u32[]{:S(2)}) copy-start(f32[16]{0:T(128)S(1)} %get-tuple-element.134) | copy-start | bytes 196
  22.9 10.1 %copy-start.66 = (f32[16]{0:T(128)}, f32[16]{0:T(128)S(1)}, u32[]{:S(2)}) copy-start(f32[16]{0:T(128)S(1)} %get-tuple-element.135) | copy-start | bytes 196
  22.9 12.3 %copy-start.64 = (f32[16]{0:T(128)}, f32[16]{0:T(128)S(1)}, u32[]{:S(2)}) copy-start(f32[16]{0:T(128)S(1)} %get-tuple-element.130) | copy-start | bytes 196
  31.9 203.6 %all-gather.7.cloned.1.call-start = ((), (), s32[]{:S(2)}) async-start(), calls=%async_computation.1 | async-start | bytes 8912896 | tf_op jit(solution)/shard_map/all_gather | solution.py:156
  32.8 5.9 %copy-start.29 = (bf16[128,8,8,128]{3,2,1,0:T(8,128)(2,1)}, bf16[128,8,8,128]{3,2,1,0:T(8,128)(2,1)S(1)}, u32[]{:S(2)}) copy-start(bf16[128,8,8,128]{3,2,1,0:T(8,128)(2,1)S(1)} %copy.195) | copy-start | bytes 6291460
  32.9 5.8 %copy-start.62 = (pred[128,128]{1,0:T(8,128)(4,1)}, pred[128,128]{1,0:T(8,128)(4,1)S(1)}, u32[]{:S(2)}) copy-start(pred[128,128]{1,0:T(8,128)(4,1)S(1)} %iota_compare_fusion) | copy-start | bytes 49156
  36.6 4.1 %copy-start.42 = (f32[8,128,16]{1,2,0:T(8,128)S(1)}, f32[8,128,16]{1,2,0:T(8,128)}, u32[]{:S(2)}) copy-start(f32[8,128,16]{1,2,0:T(8,128)} %get-tuple-element.90) | copy-start | bytes 196612
  56.0 54.3 %copy-start.91 = (pred[16]{0:T(512)(128)(4,1)}, pred[16]{0:T(512)(128)(4,1)S(1)}, u32[]{:S(2)}) copy-start(pred[16]{0:T(512)(128)(4,1)S(1)} %get-tuple-element.140) | copy-start | bytes 52
  114.9 4.0 %copy-start.24 = (f32[8,128,1,16,64]{1,4,3,0,2:T(8,128)S(1)}, f32[8,128,1,16,64]{1,4,3,0,2:T(8,128)}, u32[]{:S(2)}) copy-start(f32[8,128,1,16,64]{1,4,3,0,2:T(8,128)} %bitcast_add_fusion.1) | copy-start | bytes 12582916
  157.5 3.9 %copy-start.23 = (f32[1,16,64,128]{3,2,1,0:T(8,128)S(1)}, f32[1,16,64,128]{3,2,1,0:T(8,128)}, u32[]{:S(2)}) copy-start(f32[1,16,64,128]{3,2,1,0:T(8,128)} %get-tuple-element.69) | copy-start | bytes 1572868
  157.5 3.9 %copy-start.65 = (f32[16]{0:T(128)S(1)}, f32[16]{0:T(128)}, u32[]{:S(2)}) copy-start(f32[16]{0:T(128)} %copy-done.64) | copy-start | bytes 196
  157.6 4.8 %copy-start.21 = (f32[1,16,64,128]{3,2,1,0:T(8,128)S(1)}, f32[1,16,64,128]{3,2,1,0:T(8,128)}, u32[]{:S(2)}) copy-start(f32[1,16,64,128]{3,2,1,0:T(8,128)} %get-tuple-element.70) | copy-start | bytes 1572868
  157.6 4.8 %copy-start.75 = (f32[16]{0:T(128)S(1)}, f32[16]{0:T(128)}, u32[]{:S(2)}) copy-start(f32[16]{0:T(128)} %copy-done.74) | copy-start | bytes 196
  162.4 8.5 %copy-start.32 = (f32[1,16,64,128]{3,2,1,0:T(8,128)}, f32[1,16,64,128]{3,2,1,0:T(8,128)S(1)}, u32[]{:S(2)}) copy-start(f32[1,16,64,128]{3,2,1,0:T(8,128)S(1)} %get-tuple-element.59) | copy-start | bytes 1572868
  162.4 5.9 %copy-start.10 = (f32[8,16,64,128]{3,2,1,0:T(8,128)S(1)}, f32[8,16,64,128]{3,2,1,0:T(8,128)}, u32[]{:S(2)}) copy-start(f32[8,16,64,128]{3,2,1,0:T(8,128)} %copy-done.9) | copy-start | bytes 12582916
  163.2 7.7 %copy-start.34 = (f32[1,16,64,128]{3,2,1,0:T(8,128)}, f32[1,16,64,128]{3,2,1,0:T(8,128)S(1)}, u32[]{:S(2)}) copy-start(f32[1,16,64,128]{3,2,1,0:T(8,128)S(1)} %get-tuple-element.61) | copy-start | bytes 1572868
  164.1 6.9 %copy-start.36 = (f32[1,16,64,128]{3,2,1,0:T(8,128)}, f32[1,16,64,128]{3,2,1,0:T(8,128)S(1)}, u32[]{:S(2)}) copy-start(f32[1,16,64,128]{3,2,1,0:T(8,128)S(1)} %get-tuple-element.63) | copy-start | bytes 1572868
  164.1 4.2 %copy-start.2 = (f32[128,8,8,128]{3,2,1,0:T(8,128)S(1)}, f32[128,8,8,128]{3,2,1,0:T(8,128)}, u32[]{:S(2)}) copy-start(f32[128,8,8,128]{3,2,1,0:T(8,128)} %copy-done.1) | copy-start | bytes 12582916
  164.1 4.5 %copy-start.8 = (f32[16,64,8,128]{3,1,0,2:T(8,128)S(1)}, f32[16,64,8,128]{3,1,0,2:T(8,128)}, u32[]{:S(2)}) copy-start(f32[16,64,8,128]{3,1,0,2:T(8,128)} %get-tuple-element.137) | copy-start | bytes 12582916
  165.0 6.0 %copy-start.38 = (f32[1,16,64,128]{3,2,1,0:T(8,128)}, f32[1,16,64,128]{3,2,1,0:T(8,128)S(1)}, u32[]{:S(2)}) copy-start(f32[1,16,64,128]{3,2,1,0:T(8,128)S(1)} %get-tuple-element.65) | copy-start | bytes 1572868
  171.0 6.4 %copy-start.30 = (bf16[128,8,8,128]{3,2,1,0:T(8,128)(2,1)S(1)}, bf16[128,8,8,128]{3,2,1,0:T(8,128)(2,1)}, u32[]{:S(2)}) copy-start(bf16[128,8,8,128]{3,2,1,0:T(8,128)(2,1)} %copy-done.29) | copy-start | bytes 6291460
  177.4 12.8 %copy-start.57 = (f32[8,128,16]{1,2,0:T(8,128)S(1)}, f32[8,128,16]{1,2,0:T(8,128)}, u32[]{:S(2)}) copy-start(f32[8,128,16]{1,2,0:T(8,128)} %copy-done.56) | copy-start | bytes 196612
  177.4 12.8 %copy-start.58 = (f32[8,1,16,1]{3,2,1,0:T(8,128)S(1)}, f32[8,1,16,1]{3,2,1,0:T(8,128)}, u32[]{:S(2)}) copy-start(f32[8,1,16,1]{3,2,1,0:T(8,128)} %copy.157) | copy-start | bytes 1540
  177.4 22.9 %copy-start.44 = (f32[8,128,16]{1,2,0:T(8,128)S(1)}, f32[8,128,16]{1,2,0:T(8,128)}, u32[]{:S(2)}) copy-start(f32[8,128,16]{1,2,0:T(8,128)} %get-tuple-element.90) | copy-start | bytes 196612
  200.3 8.3 %copy-start.12 = (f32[8,128,16,64]{1,0,3,2:T(8,128)S(1)}, f32[8,128,16,64]{1,0,3,2:T(8,128)}, u32[]{:S(2)}) copy-start(f32[8,128,16,64]{1,0,3,2:T(8,128)} %copy-done.11) | copy-start | bytes 12582916
  200.3 8.3 %copy-start.33 = (f32[1,16,64,128]{3,2,1,0:T(8,128)S(1)}, f32[1,16,64,128]{3,2,1,0:T(8,128)}, u32[]{:S(2)}) copy-start(f32[1,16,64,128]{3,2,1,0:T(8,128)} %copy-done.32) | copy-start | bytes 1572868
  200.3 8.3 %copy-start.35 = (f32[1,16,64,128]{3,2,1,0:T(8,128)S(1)}, f32[1,16,64,128]{3,2,1,0:T(8,128)}, u32[]{:S(2)}) copy-start(f32[1,16,64,128]{3,2,1,0:T(8,128)} %copy-done.34) | copy-start | bytes 1572868
  200.3 8.3 %copy-start.37 = (f32[1,16,64,128]{3,2,1,0:T(8,128)S(1)}, f32[1,16,64,128]{3,2,1,0:T(8,128)}, u32[]{:S(2)}) copy-start(f32[1,16,64,128]{3,2,1,0:T(8,128)} %copy-done.36) | copy-start | bytes 1572868
  200.3 8.3 %copy-start.39 = (f32[1,16,64,128]{3,2,1,0:T(8,128)S(1)}, f32[1,16,64,128]{3,2,1,0:T(8,128)}, u32[]{:S(2)}) copy-start(f32[1,16,64,128]{3,2,1,0:T(8,128)} %copy-done.38) | copy-start | bytes 1572868
  200.3 8.3 %copy-start.41 = (f32[1,16,64,128]{3,2,1,0:T(8,128)S(1)}, f32[1,16,64,128]{3,2,1,0:T(8,128)}, u32[]{:S(2)}) copy-start(f32[1,16,64,128]{3,2,1,0:T(8,128)} %copy-done.40) | copy-start | bytes 1572868
  200.4 8.3 %copy-start.48 = (f32[1,1,16,64,128]{4,3,2,1,0:T(8,128)S(1)}, f32[1,1,16,64,128]{4,3,2,1,0:T(8,128)}, u32[]{:S(2)}) copy-start(f32[1,1,16,64,128]{4,3,2,1,0:T(8,128)} %copy-done.47) | copy-start | bytes 1572868
  200.4 8.3 %copy-start.50 = (f32[1,1,16,64,128]{4,3,2,1,0:T(8,128)S(1)}, f32[1,1,16,64,128]{4,3,2,1,0:T(8,128)}, u32[]{:S(2)}) copy-start(f32[1,1,16,64,128]{4,3,2,1,0:T(8,128)} %copy-done.49) | copy-start | bytes 1572868
  208.7 4.4 %copy-start.3 = (f32[128,8,8,128]{3,2,1,0:T(8,128)S(1)}, f32[128,8,8,128]{3,2,1,0:T(8,128)}, u32[]{:S(2)}) copy-start(f32[128,8,8,128]{3,2,1,0:T(8,128)} %copy-done.1) | copy-start | bytes 12582916
  208.7 4.4 %copy-start.46 = (f32[8,128,128]{2,1,0:T(8,128)S(1)}, f32[8,128,128]{2,1,0:T(8,128)}, u32[]{:S(2)}) copy-start(f32[8,128,128]{2,1,0:T(8,128)} %copy-done.45) | copy-start | bytes 1572868
  208.7 4.4 %copy-start.55 = (f32[8,128,16]{1,2,0:T(8,128)S(1)}, f32[8,128,16]{1,2,0:T(8,128)}, u32[]{:S(2)}) copy-start(f32[8,128,16]{1,2,0:T(8,128)} %copy-done.54) | copy-start | bytes 196612
  208.7 4.4 %copy-start.63 = (pred[128,128]{1,0:T(8,128)(4,1)S(1)}, pred[128,128]{1,0:T(8,128)(4,1)}, u32[]{:S(2)}) copy-start(pred[128,128]{1,0:T(8,128)(4,1)} %copy-done.62) | copy-start | bytes 49156
  208.7 4.4 %copy-start.94 = (f32[8,16,64,128]{3,2,1,0:T(8,128)S(1)}, f32[8,16,64,128]{3,2,1,0:T(8,128)}, u32[]{:S(2)}) copy-start(f32[8,16,64,128]{3,2,1,0:T(8,128)} %get-tuple-element.139) | copy-start | bytes 12582916
  213.1 7.5 %copy-start.53 = (f32[8,128,1,16]{1,0,3,2:T(8,128)S(1)}, f32[8,128,1,16]{1,0,3,2:T(8,128)}, u32[]{:S(2)}) copy-start(f32[8,128,1,16]{1,0,3,2:T(8,128)} %copy.159) | copy-start | bytes 196612
  220.6 4.1 %copy-start.15 = (bf16[1024,1024]{0,1:T(8,128)(2,1)S(1)}, bf16[1024,1024]{0,1:T(8,128)(2,1)}, u32[]{:S(2)}) copy-start(bf16[1024,1024]{0,1:T(8,128)(2,1)} %get-tuple-element.79) | copy-start | bytes 6291460
  220.7 6.6 %copy-start.59 = (f32[16,16]{1,0:T(8,128)S(1)}, f32[16,16]{1,0:T(8,128)}, u32[]{:S(2)}) copy-start(f32[16,16]{1,0:T(8,128)} %get-tuple-element.54) | copy-start | bytes 3076
  220.7 6.6 %copy-start.92 = (pred[16]{0:T(512)(128)(4,1)S(1)}, pred[16]{0:T(512)(128)(4,1)}, u32[]{:S(2)}) copy-start(pred[16]{0:T(512)(128)(4,1)} %copy-done.91) | copy-start | bytes 52
  227.4 16.6 %copy-start.78 = (f32[16]{0:T(128)}, f32[16]{0:T(128)S(1)}, u32[]{:S(2)}) copy-start(f32[16]{0:T(128)S(1)} %get-tuple-element.96) | copy-start | bytes 196
  227.4 16.6 %copy-start.79 = (f32[16]{0:T(128)}, f32[16]{0:T(128)S(1)}, u32[]{:S(2)}) copy-start(f32[16]{0:T(128)S(1)} %get-tuple-element.97) | copy-start | bytes 196
  227.4 16.6 %copy-start.80 = (f32[16]{0:T(128)}, f32[16]{0:T(128)S(1)}, u32[]{:S(2)}) copy-start(f32[16]{0:T(128)S(1)} %get-tuple-element.98) | copy-start | bytes 196
  227.5 16.6 %copy-start.81 = (f32[16]{0:T(128)}, f32[16]{0:T(128)S(1)}, u32[]{:S(2)}) copy-start(f32[16]{0:T(128)S(1)} %get-tuple-element.99) | copy-start | bytes 196
  227.5 16.6 %copy-start.82 = (f32[16]{0:T(128)}, f32[16]{0:T(128)S(1)}, u32[]{:S(2)}) copy-start(f32[16]{0:T(128)S(1)} %get-tuple-element.100) | copy-start | bytes 196
  227.5 16.6 %copy-start.83 = (f32[16]{0:T(128)}, f32[16]{0:T(128)S(1)}, u32[]{:S(2)}) copy-start(f32[16]{0:T(128)S(1)} %get-tuple-element.101) | copy-start | bytes 196
  227.5 16.6 %copy-start.84 = (f32[16]{0:T(128)}, f32[16]{0:T(128)S(1)}, u32[]{:S(2)}) copy-start(f32[16]{0:T(128)S(1)} %get-tuple-element.102) | copy-start | bytes 196
  227.5 16.6 %copy-start.85 = (f32[16]{0:T(128)}, f32[16]{0:T(128)S(1)}, u32[]{:S(2)}) copy-start(f32[16]{0:T(128)S(1)} %get-tuple-element.103) | copy-start | bytes 196
  227.5 16.6 %copy-start.86 = (f32[16]{0:T(128)}, f32[16]{0:T(128)S(1)}, u32[]{:S(2)}) copy-start(f32[16]{0:T(128)S(1)} %get-tuple-element.104) | copy-start | bytes 196
  227.5 16.6 %copy-start.87 = (f32[16]{0:T(128)}, f32[16]{0:T(128)S(1)}, u32[]{:S(2)}) copy-start(f32[16]{0:T(128)S(1)} %get-tuple-element.105) | copy-start | bytes 196
  227.5 16.6 %copy-start.88 = (f32[16]{0:T(128)}, f32[16]{0:T(128)S(1)}, u32[]{:S(2)}) copy-start(f32[16]{0:T(128)S(1)} %get-tuple-element.106) | copy-start | bytes 196
  227.5 16.6 %copy-start.89 = (f32[16]{0:T(128)}, f32[16]{0:T(128)S(1)}, u32[]{:S(2)}) copy-start(f32[16]{0:T(128)S(1)} %get-tuple-element.107) | copy-start | bytes 196
  235.5 7.2 %copy-start.31 = (f32[8,128,128]{2,1,0:T(8,128)S(1)}, f32[8,128,128]{2,1,0:T(8,128)}, u32[]{:S(2)}) copy-start(f32[8,128,128]{2,1,0:T(8,128)} %get-tuple-element.42) | copy-start | bytes 1572868
  235.5 7.2 %copy-start.51 = (f32[8,128,1,128]{1,3,0,2:T(8,128)S(1)}, f32[8,128,1,128]{1,3,0,2:T(8,128)}, u32[]{:S(2)}) copy-start(f32[8,128,1,128]{1,3,0,2:T(8,128)} %fusion.74) | copy-start | bytes 1572868
  257.9 4.3 %copy-start.93 = (f32[16]{0:T(128)S(1)}, f32[16]{0:T(128)}, u32[]{:S(2)}) copy-start(f32[16]{0:T(128)} %get-tuple-element.50) | copy-start | bytes 196
  257.9 5.2 %copy-start.14 = (f32[1024,1,16,64]{0,3,2,1:T(8,128)S(1)}, f32[1024,1,16,64]{0,3,2,1:T(8,128)}, u32[]{:S(2)}) copy-start(f32[1024,1,16,64]{0,3,2,1:T(8,128)} %get-tuple-element.83) | copy-start | bytes 12582916
  (33 other events, 85.0 us)
Sparse Core Ops, SparseCore 0:
  32.0 78.1 all-gather.4
  157.6 68.0 all-gather.6
